TPU v7x, 256 devices: a whole 4x4x8 slice. The times are simulated.
256 devices in a mesh: shot: 32 (over y, z_hi, core), depth: 8 (over x, z_lo).
Axes of the slice: x: 4, y: 4, z: 8 (z_hi: 4, z_lo: 2; z = z_hi * 2 + z_lo), core: 2. Of those that a mesh axis runs over, the one named last changes fastest.
Arguments:
- forward_start: bfloat16 [2, 32, 128, 128, 128], P(None, 'shot', 'depth'), may hold values from -6 to 6
- adjoint_end: bfloat16 [2, 32, 128, 128, 128], P(None, 'shot', 'depth'), may hold values from -6 to 6
- velocity: float32 [128, 128, 128], P('depth'), may hold values from 1.5 to 4.5
- source_cell: int32 [32], P('shot'), may hold values from 0 to 2097151
- wavelet: float32 [32, 4], P('shot'), may hold values from -16 to 16
- receiver_cell: int32 [32, 1024], P('shot'), may hold values from 0 to 2097151
- observed: float32 [32, 4, 1024], P('shot'), may hold values from -16 to 16
Outputs:
- forward_end: bfloat16 [2, 32, 128, 128, 128], P(None, 'shot', 'depth')
- adjoint_start: bfloat16 [2, 32, 128, 128, 128], P(None, 'shot', 'depth')
- velocity_new: float32 [128, 128, 128], P('depth')
All inputs are finite; a program needn't handle non-finite values.
Results may differ from a plain program's by a relative error of at most 0.0079.
Values may be sent and summed in bfloat16 or wider, within the bound.
No kernel may reach another device: no remote copies, remote signals or barrier semaphores. Data moves between devices by JAX's collectives and lax.ppermute only.
A program may use at most 64 MiB of HBM per device.

v0:
```python
import math
import jax
import jax.numpy as jnp
from jax import lax
from jax.sharding import PartitionSpec as P

CZ = 16
NX = 128
NY = 128
STEPS = 4
stencil_weights = (1.6, -0.2, 8.0 / 315.0, -1.0 / 560.0)
center_weight = -205.0 / 72.0
courant = 0.095
step_base = 0.01
low_speed = 1.5
high_speed = 4.5


def padded_2(cells, sides, width):
    for axis, dim in sides:
        count = lax.axis_size(axis)
        ends = count - 1
        head = lax.slice_in_dim(cells, 0, width, axis=dim)
        tail = lax.slice_in_dim(cells, cells.shape[dim] - width, cells.shape[dim], axis=dim)
        cells = jnp.concatenate(
            [
                lax.ppermute(tail, axis, [(i, (i + 1) % count) for i in range(ends)]),
                cells,
                lax.ppermute(head, axis, [((i + 1) % count, i) for i in range(ends)]),
            ],
            axis=dim,
        )
    return cells


def laplace(depth_padded):
    padded = jnp.pad(depth_padded, ((0, 0), (0, 0), (4, 4), (4, 4)))
    depth_len = padded.shape[1] - 8
    row_len = padded.shape[2] - 8
    column_len = padded.shape[3] - 8

    def window(along_z, along_x, along_y):
        return padded[
            :,
            4 + along_z : 4 + along_z + depth_len,
            4 + along_x : 4 + along_x + row_len,
            4 + along_y : 4 + along_y + column_len,
        ]

    summed = 3.0 * center_weight * window(0, 0, 0)
    for offset in range(1, 5):
        weight = stencil_weights[offset - 1]
        summed = summed + weight * (
            window(offset, 0, 0)
            + window(-offset, 0, 0)
            + window(0, offset, 0)
            + window(0, -offset, 0)
            + window(0, 0, offset)
            + window(0, 0, -offset)
        )
    return summed


def inject(wavefield, cell_ids, values, anchor):
    shot_count = wavefield.shape[0]
    depth_len = wavefield.shape[1]
    plane_size = NX * NY
    planes = cell_ids // plane_size - anchor
    owned_mask = (planes >= 0) & (planes < depth_len)
    flat_index = jnp.clip(planes, 0, depth_len - 1) * plane_size + cell_ids % plane_size
    rows_index = jnp.broadcast_to(jnp.arange(shot_count, dtype=jnp.int32)[:, None], cell_ids.shape)
    flattened = (
        wavefield.reshape(shot_count, -1)
        .at[rows_index, flat_index]
        .add(jnp.where(owned_mask, values, 0.0))
    )
    return flattened.reshape(wavefield.shape)


def record(wavefield, cell_ids, anchor):
    shot_count = wavefield.shape[0]
    plane_size = NX * NY
    planes = cell_ids // plane_size - anchor
    flat_index = jnp.clip(planes, 0, wavefield.shape[1] - 1) * plane_size + cell_ids % plane_size
    return jnp.take_along_axis(wavefield.reshape(shot_count, -1), flat_index, axis=1).astype(
        jnp.float32
    )


def body(forward_start, adjoint_end, velocity, source_cell, wavelet, receiver_cell, observed):
    anchor = lax.axis_index("depth") * CZ
    wave_model = (courant * velocity) ** 2
    source_ids = source_cell[:, None]
    images = []
    residuals = []
    earlier = forward_start[0]
    current = forward_start[1]
    for moment in range(STEPS):
        padded = padded_2(current, (("depth", 1),), 4)
        laplacian = laplace(padded.astype(jnp.float32))
        updated = (
            2.0 * current.astype(jnp.float32) - earlier.astype(jnp.float32) + wave_model * laplacian
        )
        updated = inject(updated, source_ids, wavelet[:, moment : moment + 1], anchor).astype(
            jnp.bfloat16
        )
        images.append(laplacian.astype(jnp.bfloat16))
        residuals.append(record(updated, receiver_cell, anchor) - observed[:, moment])
        earlier, current = (current, updated)
    images = list(lax.optimization_barrier(tuple(images)))
    nearer = adjoint_end[0]
    farther = adjoint_end[1]
    gradient = jnp.zeros(velocity.shape, jnp.float32)
    for moment in reversed(range(STEPS)):
        padded = padded_2(nearer, (("depth", 1),), 4)
        laplacian = laplace(padded.astype(jnp.float32))
        updated = (
            2.0 * nearer.astype(jnp.float32) - farther.astype(jnp.float32) + wave_model * laplacian
        )
        updated = inject(updated, receiver_cell, residuals[moment], anchor).astype(jnp.bfloat16)
        gradient = gradient + jnp.sum(
            updated.astype(jnp.float32) * images[moment].astype(jnp.float32), axis=0
        )
        farther, nearer = (nearer, updated)
    step_scale = step_base / math.sqrt(forward_start.shape[1] * lax.axis_size("shot"))
    summed = lax.psum(gradient, "shot")
    velocity_new = jnp.clip(velocity - step_scale * summed, low_speed, high_speed)
    forward_end = jnp.stack([earlier, current])
    adjoint_start = jnp.stack([nearer, farther])
    return (forward_end, adjoint_start, velocity_new)


def solution(mesh):
    placed = (
        P(None, "shot", "depth", None, None),
        P(None, "shot", "depth", None, None),
        P("depth", None, None),
        P("shot"),
        P("shot", None),
        P("shot", None),
        P("shot", None, None),
    )
    return jax.shard_map(
        body,
        mesh=mesh,
        in_specs=placed,
        out_specs=(
            P(None, "shot", "depth", None, None),
            P(None, "shot", "depth", None, None),
            P("depth", None, None),
        ),
        check_vma=False,
    )
```

profile of v0, /device:TPU:1, one launch (start us, length us, event | category | flops | bytes accessed | tf_op | source)
XLA Modules:
  0.0 539.6 jit_solution(1244440493901960534)
XLA Ops:
  7.3 1.2 slice_bitcast_fusion.1
  8.5 4.4 collective-permute-start
  12.8 1.3 collective-permute-start.1
  14.2 0.8 copy-done.20
  15.0 0.7 fusion.229
  15.7 4.0 collective-permute-start.8
  19.7 1.3 collective-permute-start.9
  21.2 0.7 fusion.234
  25.0 0.8 and_reduce_fusion.1
  26.1 3.0 fusion.223
  29.4 0.6 fusion.235
  32.0 10.9 %convert_reduce_fusion.3 = bf16[262144]{0:T(1024)(128)(2,1)S(1)} fusion(f32[1,262144]{1,0:T(1,128)S(1)} %scatter-add.48), kind=kLoop, calls=%fused_computation.413 | loop fusion | flops 262144 | bytes 1572864 | tf_op jit(solution)/shard_map/convert_element_type | solution.py:104
  42.9 4.2 collective-permute-start.2
  47.1 1.3 collective-permute-start.3
  48.4 0.6 collective-permute-done.2
  49.0 5.8 %collective-permute-done.3 = bf16[1,4,128,128]{3,2,1,0:T(8,128)(2,1)S(1)} collective-permute-done((bf16[1,4,128,128]{3,2,1,0:T(8,128)(2,1)S(1)}, bf16[1,4,128,128]{3,2,1,0:T(8,128)(2,1)S(1)}, u32[]{:S(2)}, u32[]{:S(2)}) %collective-permute-start.3) | collective-permute-done | bytes 131104 | tf_op jit(solution)/shard_map/ppermute | solution.py:29
  54.9 3.1 fusion.221
  58.3 0.6 fusion.236
  60.7 0.6 scatter-add.49
  61.3 10.9 %convert_reduce_fusion.2 = bf16[262144]{0:T(1024)(128)(2,1)S(1)} fusion(f32[1,262144]{1,0:T(1,128)S(1)} %scatter-add.49), kind=kLoop, calls=%fused_computation.412 | loop fusion | flops 262144 | bytes 1572864 | tf_op jit(solution)/shard_map/convert_element_type | solution.py:104
  72.2 3.2 collective-permute-start.4
  75.4 1.3 collective-permute-start.5
  76.7 11.4 %gather_fusion.3 = bf16[1024]{0:T(1024)(128)(2,1)} fusion(bf16[262144]{0:T(1024)(128)(2,1)S(1)} %convert_reduce_fusion.3, s32[1024]{0:T(1024)S(1)} %broadcast_clamp_fusion), kind=kCustom, calls=%fused_computation.3.clone | custom fusion | bytes 8192 | tf_op jit(solution)/shard_map/jit(take_along_axis)/gather | solution.py:85
  88.3 3.1 fusion.219
  91.6 0.7 fusion.237
  94.3 10.9 %convert_reduce_fusion.1 = bf16[262144]{0:T(1024)(128)(2,1)S(1)} fusion(f32[1,262144]{1,0:T(1,128)S(1)} %scatter-add.50), kind=kLoop, calls=%fused_computation.411 | loop fusion | flops 262144 | bytes 1572864 | tf_op jit(solution)/shard_map/convert_element_type | solution.py:104
  105.2 0.7 fusion.230
  105.9 4.0 collective-permute-start.6
  109.9 1.5 collective-permute-start.7
  111.4 1.2 maximum_convert_fusion.4
  112.6 13.5 %gather_fusion.2 = bf16[1024]{0:T(1024)(128)(2,1)S(1)} fusion(bf16[262144]{0:T(1024)(128)(2,1)} %copy-done.1, s32[1024]{0:T(1024)S(1)} %broadcast_clamp_fusion), kind=kCustom, calls=%fused_computation.2.clone | custom fusion | bytes 8192 | tf_op jit(solution)/shard_map/jit(take_along_axis)/gather | solution.py:85
  126.1 6.8 %gather_fusion.1 = bf16[1024]{0:T(1024)(128)(2,1)S(1)} fusion(bf16[262144]{0:T(1024)(128)(2,1)S(1)} %convert_reduce_fusion.1, s32[1024]{0:T(1024)S(1)} %broadcast_clamp_fusion), kind=kCustom, calls=%fused_computation.1.clone | custom fusion | bytes 8192 | tf_op jit(solution)/shard_map/jit(take_along_axis)/gather | solution.py:85
  132.9 1.0 maximum_convert_fusion.3
  134.0 3.1 fusion.217
  137.0 3.4 fusion.6
  140.5 1.0 copy-done.14
  141.4 0.6 fusion.238
  143.9 1.3 scatter-add.51
  145.2 12.0 %convert_reduce_fusion = bf16[262144]{0:T(1024)(128)(2,1)S(1)} fusion(f32[1,262144]{1,0:T(1,128)} %scatter-add.51), kind=kLoop, calls=%fused_computation.410 | loop fusion | flops 262144 | bytes 1572864 | tf_op jit(solution)/shard_map/convert_element_type | solution.py:104
  157.1 6.8 %gather_fusion = bf16[1024]{0:T(1024)(128)(2,1)S(1)} fusion(bf16[262144]{0:T(1024)(128)(2,1)S(1)} %convert_reduce_fusion, s32[1024]{0:T(1024)S(1)} %broadcast_clamp_fusion), kind=kCustom, calls=%fused_computation.clone | custom fusion | bytes 8192 | tf_op jit(solution)/shard_map/jit(take_along_axis)/gather | solution.py:85
  164.0 6.5 %scatter_fusion = f32[262144]{0:T(1024)S(1)} fusion(f32[262144]{0:T(1024)S(1)} %bitcast.100, s32[1024]{0:T(1024)S(1)} %broadcast_select_fusion, f32[1024]{0:T(1024)S(1)} %bitcast.136), kind=kCustom, calls=%fused_computation.4 | custom fusion | flops 1024 | bytes 16384
  170.6 4.9 collective-permute-start.10
  175.6 1.3 collective-permute-start.11
  176.9 0.6 collective-permute-done.10
  177.5 4.7 collective-permute-done.11
  182.3 2.4 fusion.7
  184.7 6.7 %scatter_fusion.1 = f32[262144]{0:T(1024)S(1)} fusion(f32[262144]{0:T(1024)S(1)} %bitcast.102, s32[1024]{0:T(1024)S(1)} %broadcast_select_fusion, f32[1024]{0:T(1024)S(1)} %bitcast.135), kind=kCustom, calls=%fused_computation.5 | custom fusion | flops 1024 | bytes 16384
  191.5 5.5 %collective-permute-start.12 = (bf16[1,4,128,128]{3,2,1,0:T(8,128)(2,1)S(1)}, bf16[1,4,128,128]{3,2,1,0:T(8,128)(2,1)S(1)}, u32[]{:S(2)}, u32[]{:S(2)}) collective-permute-start(bf16[1,4,128,128]{3,2,1,0:T(8,128)(2,1)S(1)} %get-tuple-element.74), channel_id=1, source_target_pairs={{0,1},{1,2},{2,3},{3,4},{4,5},{5,6},{6,7},{8,9},{9,10},{10,11},{11... | collective-permute-start | bytes 393224 | tf_op jit(solution)/shard_map/ppermute | solution.py:27
  197.0 1.3 collective-permute-start.13
  198.3 0.6 collective-permute-done.12
  198.9 4.8 collective-permute-done.13
  203.9 2.4 fusion.11
  206.3 6.5 %scatter_fusion.2 = f32[262144]{0:T(1024)S(1)} fusion(f32[262144]{0:T(1024)S(1)} %bitcast.103, s32[1024]{0:T(1024)S(1)} %broadcast_select_fusion, f32[1024]{0:T(1024)S(1)} %bitcast.134), kind=kCustom, calls=%fused_computation.6 | custom fusion | flops 1024 | bytes 16384
  212.9 1.9 collective-permute-start.14
  214.8 1.3 collective-permute-start.15
  216.1 0.6 collective-permute-done.14
  216.8 4.8 collective-permute-done.15
  221.7 2.4 fusion.13
  224.2 6.5 %scatter_fusion.3 = f32[262144]{0:T(1024)S(1)} fusion(f32[262144]{0:T(1024)S(1)} %bitcast.101, s32[1024]{0:T(1024)S(1)} %broadcast_select_fusion, f32[1024]{0:T(1024)S(1)} %bitcast.133), kind=kCustom, calls=%fused_computation.7 | custom fusion | flops 1024 | bytes 16384
  230.7 0.8 copy-done.13
  232.2 3.2 fusion.10
  235.4 2.5 pad_maximum_fusion
  237.9 292.2 %all-reduce.11.cloned.1.call-done = f32[16,128,128]{2,1,0:T(8,128)} async-done(((f32[16,128,128]{2,1,0:T(8,128)}), f32[16,128,128]{2,1,0:T(8,128)}) %all-reduce.11.cloned.1.call-update) | async-done | bytes 1048592 | tf_op jit(solution)/shard_map/psum | solution.py:126
  530.1 2.4 subtract_clamp_fusion
  (89 shorter events, 3.3 us)
Async XLA Ops:
  7.2 13.9 %copy-start.26 = (s32[2]{0:T(128)S(1)}, s32[2]{0:T(128)}, u32[]{:S(2)}) copy-start(s32[2]{0:T(128)} %constant.279) | copy-start | bytes 28
  7.2 18.6 %copy-start.25 = (s32[2]{0:T(128)S(1)}, s32[2]{0:T(128)}, u32[]{:S(2)}) copy-start(s32[2]{0:T(128)} %constant.276) | copy-start | bytes 28
  7.2 6.9 %copy-start.15 = (bf16[2,1,16,128,128]{4,3,2,1,0:T(8,128)(2,1)S(1)}, bf16[2,1,16,128,128]{4,3,2,1,0:T(8,128)(2,1)}, u32[]{:S(2)}) copy-start(bf16[2,1,16,128,128]{4,3,2,1,0:T(8,128)(2,1)} %param.18) | copy-start | bytes 3145732
  7.2 13.8 %copy-start.24 = (s32[1,1024]{1,0:T(1,128)S(1)}, s32[1,1024]{1,0:T(1,128)}, u32[]{:S(2)}) copy-start(s32[1,1024]{1,0:T(1,128)} %param.22) | copy-start | bytes 12292
  7.2 14.0 %copy-start.23 = (f32[1,4]{1,0:T(1,128)S(1)}, f32[1,4]{1,0:T(1,128)}, u32[]{:S(2)}) copy-start(f32[1,4]{1,0:T(1,128)} %param.21) | copy-start | bytes 52
  7.2 522.9 %all-reduce.11.cloned.1.call-start = ((), (), s32[]{:S(2)}) async-start(), calls=%async_computation | async-start | bytes 2097152 | tf_op jit(solution)/shard_map/psum | solution.py:126
  8.5 17.4 %collective-permute-start = (bf16[1,4,128,128]{3,2,1,0:T(8,128)(2,1)S(1)}, bf16[1,4,128,128]{3,2,1,0:T(8,128)(2,1)S(1)}, u32[]{:S(2)}, u32[]{:S(2)}) collective-permute-start(bf16[1,4,128,128]{3,2,1,0:T(8,128)(2,1)S(1)} %get-tuple-element.86), channel_id=1, source_target_pairs={{0,1},{1,2},{2,3},{3,4},{4,5},{5,6},{6,7},{8,9},{9,10},{10,11},{11... | collective-permute-start | bytes 393224 | tf_op jit(solution)/shard_map/ppermute | solution.py:27
  12.8 13.1 %collective-permute-start.1 = (bf16[1,4,128,128]{3,2,1,0:T(8,128)(2,1)S(1)}, bf16[1,4,128,128]{3,2,1,0:T(8,128)(2,1)S(1)}, u32[]{:S(2)}, u32[]{:S(2)}) collective-permute-start(bf16[1,4,128,128]{3,2,1,0:T(8,128)(2,1)S(1)} %get-tuple-element.87), channel_id=1, source_target_pairs={{1,0},{2,1},{3,2},{4,3},{5,4},{6,5},{7,6},{9,8},{10,9},{11,10},{12... | collective-permute-start | bytes 393224 | tf_op jit(solution)/shard_map/ppermute | solution.py:29
  14.2 0.8 copy-start.20
  15.7 95.7 %collective-permute-start.8 = (bf16[1,4,128,128]{3,2,1,0:T(8,128)(2,1)}, bf16[1,4,128,128]{3,2,1,0:T(8,128)(2,1)S(1)}, u32[]{:S(2)}, u32[]{:S(2)}) collective-permute-start(bf16[1,4,128,128]{3,2,1,0:T(8,128)(2,1)} %get-tuple-element.78), channel_id=1, source_target_pairs={{0,1},{1,2},{2,3},{3,4},{4,5},{5,6},{6,7},{8,9},{9,10},{10,11},{11... | collective-permute-start | bytes 393224 | tf_op jit(solution)/shard_map/ppermute | solution.py:27
  19.7 91.7 %collective-permute-start.9 = (bf16[1,4,128,128]{3,2,1,0:T(8,128)(2,1)}, bf16[1,4,128,128]{3,2,1,0:T(8,128)(2,1)S(1)}, u32[]{:S(2)}, u32[]{:S(2)}) collective-permute-start(bf16[1,4,128,128]{3,2,1,0:T(8,128)(2,1)} %get-tuple-element.79), channel_id=1, source_target_pairs={{1,0},{2,1},{3,2},{4,3},{5,4},{6,5},{7,6},{9,8},{10,9},{11,10},{12... | collective-permute-start | bytes 393224 | tf_op jit(solution)/shard_map/ppermute | solution.py:29
  26.0 3.1 copy-start
  26.1 3.1 copy-start.18
  42.9 6.1 %collective-permute-start.2 = (bf16[1,4,128,128]{3,2,1,0:T(8,128)(2,1)S(1)}, bf16[1,4,128,128]{3,2,1,0:T(8,128)(2,1)S(1)}, u32[]{:S(2)}, u32[]{:S(2)}) collective-permute-start(bf16[1,4,128,128]{3,2,1,0:T(8,128)(2,1)S(1)} %get-tuple-element.84), channel_id=1, source_target_pairs={{0,1},{1,2},{2,3},{3,4},{4,5},{5,6},{6,7},{8,9},{9,10},{10,11},{11... | collective-permute-start | bytes 393224 | tf_op jit(solution)/shard_map/ppermute | solution.py:27
  47.1 7.7 %collective-permute-start.3 = (bf16[1,4,128,128]{3,2,1,0:T(8,128)(2,1)S(1)}, bf16[1,4,128,128]{3,2,1,0:T(8,128)(2,1)S(1)}, u32[]{:S(2)}, u32[]{:S(2)}) collective-permute-start(bf16[1,4,128,128]{3,2,1,0:T(8,128)(2,1)S(1)} %get-tuple-element.85), channel_id=1, source_target_pairs={{1,0},{2,1},{3,2},{4,3},{5,4},{6,5},{7,6},{9,8},{10,9},{11,10},{12... | collective-permute-start | bytes 393224 | tf_op jit(solution)/shard_map/ppermute | solution.py:29
  54.9 3.1 copy-start.19
  72.2 19.2 %copy-start.1 = (bf16[262144]{0:T(1024)(128)(2,1)}, bf16[262144]{0:T(1024)(128)(2,1)S(1)}, u32[]{:S(2)}) copy-start(bf16[262144]{0:T(1024)(128)(2,1)S(1)} %convert_reduce_fusion.2) | copy-start | bytes 1572868
  72.2 15.9 %collective-permute-start.4 = (bf16[1,4,128,128]{3,2,1,0:T(8,128)(2,1)S(1)}, bf16[1,4,128,128]{3,2,1,0:T(8,128)(2,1)S(1)}, u32[]{:S(2)}, u32[]{:S(2)}) collective-permute-start(bf16[1,4,128,128]{3,2,1,0:T(8,128)(2,1)S(1)} %get-tuple-element.82), channel_id=1, source_target_pairs={{0,1},{1,2},{2,3},{3,4},{4,5},{5,6},{6,7},{8,9},{9,10},{10,11},{11... | collective-permute-start | bytes 393224 | tf_op jit(solution)/shard_map/ppermute | solution.py:27
  75.4 12.7 %collective-permute-start.5 = (bf16[1,4,128,128]{3,2,1,0:T(8,128)(2,1)S(1)}, bf16[1,4,128,128]{3,2,1,0:T(8,128)(2,1)S(1)}, u32[]{:S(2)}, u32[]{:S(2)}) collective-permute-start(bf16[1,4,128,128]{3,2,1,0:T(8,128)(2,1)S(1)} %get-tuple-element.83), channel_id=1, source_target_pairs={{1,0},{2,1},{3,2},{4,3},{5,4},{6,5},{7,6},{9,8},{10,9},{11,10},{12... | collective-permute-start | bytes 393224 | tf_op jit(solution)/shard_map/ppermute | solution.py:29
  105.9 27.0 %collective-permute-start.6 = (bf16[1,4,128,128]{3,2,1,0:T(8,128)(2,1)}, bf16[1,4,128,128]{3,2,1,0:T(8,128)(2,1)S(1)}, u32[]{:S(2)}, u32[]{:S(2)}) collective-permute-start(bf16[1,4,128,128]{3,2,1,0:T(8,128)(2,1)} %get-tuple-element.80), channel_id=1, source_target_pairs={{0,1},{1,2},{2,3},{3,4},{4,5},{5,6},{6,7},{8,9},{9,10},{10,11},{11... | collective-permute-start | bytes 393224 | tf_op jit(solution)/shard_map/ppermute | solution.py:27
  109.9 23.0 %collective-permute-start.7 = (bf16[1,4,128,128]{3,2,1,0:T(8,128)(2,1)}, bf16[1,4,128,128]{3,2,1,0:T(8,128)(2,1)}, u32[]{:S(2)}, u32[]{:S(2)}) collective-permute-start(bf16[1,4,128,128]{3,2,1,0:T(8,128)(2,1)} %get-tuple-element.81), channel_id=1, source_target_pairs={{1,0},{2,1},{3,2},{4,3},{5,4},{6,5},{7,6},{9,8},{10,9},{11,10},{12... | collective-permute-start | bytes 393224 | tf_op jit(solution)/shard_map/ppermute | solution.py:29
  133.9 3.1 copy-start.2
  133.9 3.1 copy-start.16
  140.5 1.0 copy-start.14
  145.1 18.8 %copy-start.21 = (f32[1,4,1024]{2,1,0:T(4,128)S(1)}, f32[1,4,1024]{2,1,0:T(4,128)}, u32[]{:S(2)}) copy-start(f32[1,4,1024]{2,1,0:T(4,128)} %param.23) | copy-start | bytes 49156
  145.2 18.8 %copy-start.22 = (bf16[1024]{0:T(1024)(128)(2,1)S(1)}, bf16[1024]{0:T(1024)(128)(2,1)}, u32[]{:S(2)}) copy-start(bf16[1024]{0:T(1024)(128)(2,1)} %gather_fusion.3) | copy-start | bytes 6148
  145.2 18.9 %copy-start.3 = (f32[1,16,128,128]{3,2,1,0:T(8,128)S(1)}, f32[1,16,128,128]{3,2,1,0:T(8,128)}, u32[]{:S(2)}) copy-start(f32[1,16,128,128]{3,2,1,0:T(8,128)} %get-tuple-element.70) | copy-start | bytes 3145732
  170.6 14.1 %copy-start.4 = (bf16[262144]{0:T(1024)(128)(2,1)}, bf16[262144]{0:T(1024)(128)(2,1)S(1)}, u32[]{:S(2)}) copy-start(bf16[262144]{0:T(1024)(128)(2,1)S(1)} %convert_element_type.608) | copy-start | bytes 1572868
  170.6 11.7 %copy-start.17 = (bf16[2,1,16,128,128]{4,3,2,1,0:T(8,128)(2,1)S(1)}, bf16[2,1,16,128,128]{4,3,2,1,0:T(8,128)(2,1)}, u32[]{:S(2)}) copy-start(bf16[2,1,16,128,128]{4,3,2,1,0:T(8,128)(2,1)} %param.18) | copy-start | bytes 3145732
  170.6 6.9 %collective-permute-start.10 = (bf16[1,4,128,128]{3,2,1,0:T(8,128)(2,1)S(1)}, bf16[1,4,128,128]{3,2,1,0:T(8,128)(2,1)S(1)}, u32[]{:S(2)}, u32[]{:S(2)}) collective-permute-start(bf16[1,4,128,128]{3,2,1,0:T(8,128)(2,1)S(1)} %get-tuple-element.76), channel_id=1, source_target_pairs={{0,1},{1,2},{2,3},{3,4},{4,5},{5,6},{6,7},{8,9},{9,10},{10,11},{11... | collective-permute-start | bytes 393224 | tf_op jit(solution)/shard_map/ppermute | solution.py:27
  175.6 6.6 %collective-permute-start.11 = (bf16[1,4,128,128]{3,2,1,0:T(8,128)(2,1)S(1)}, bf16[1,4,128,128]{3,2,1,0:T(8,128)(2,1)S(1)}, u32[]{:S(2)}, u32[]{:S(2)}) collective-permute-start(bf16[1,4,128,128]{3,2,1,0:T(8,128)(2,1)S(1)} %get-tuple-element.77), channel_id=1, source_target_pairs={{1,0},{2,1},{3,2},{4,3},{5,4},{6,5},{7,6},{9,8},{10,9},{11,10},{12... | collective-permute-start | bytes 393224 | tf_op jit(solution)/shard_map/ppermute | solution.py:29
  191.5 14.8 %copy-start.7 = (bf16[262144]{0:T(1024)(128)(2,1)}, bf16[262144]{0:T(1024)(128)(2,1)S(1)}, u32[]{:S(2)}) copy-start(bf16[262144]{0:T(1024)(128)(2,1)S(1)} %convert_element_type.609) | copy-start | bytes 1572868
  191.5 12.4 %copy-start.5 = (bf16[262144]{0:T(1024)(128)(2,1)S(1)}, bf16[262144]{0:T(1024)(128)(2,1)}, u32[]{:S(2)}) copy-start(bf16[262144]{0:T(1024)(128)(2,1)} %copy-done.4) | copy-start | bytes 1572868
  191.5 7.4 %collective-permute-start.12 = (bf16[1,4,128,128]{3,2,1,0:T(8,128)(2,1)S(1)}, bf16[1,4,128,128]{3,2,1,0:T(8,128)(2,1)S(1)}, u32[]{:S(2)}, u32[]{:S(2)}) collective-permute-start(bf16[1,4,128,128]{3,2,1,0:T(8,128)(2,1)S(1)} %get-tuple-element.74), channel_id=1, source_target_pairs={{0,1},{1,2},{2,3},{3,4},{4,5},{5,6},{6,7},{8,9},{9,10},{10,11},{11... | collective-permute-start | bytes 393224 | tf_op jit(solution)/shard_map/ppermute | solution.py:27
  197.0 6.7 %collective-permute-start.13 = (bf16[1,4,128,128]{3,2,1,0:T(8,128)(2,1)S(1)}, bf16[1,4,128,128]{3,2,1,0:T(8,128)(2,1)S(1)}, u32[]{:S(2)}, u32[]{:S(2)}) collective-permute-start(bf16[1,4,128,128]{3,2,1,0:T(8,128)(2,1)S(1)} %get-tuple-element.75), channel_id=1, source_target_pairs={{1,0},{2,1},{3,2},{4,3},{5,4},{6,5},{7,6},{9,8},{10,9},{11,10},{12... | collective-permute-start | bytes 393224 | tf_op jit(solution)/shard_map/ppermute | solution.py:29
  212.8 11.3 %copy-start.10 = (bf16[262144]{0:T(1024)(128)(2,1)}, bf16[262144]{0:T(1024)(128)(2,1)S(1)}, u32[]{:S(2)}) copy-start(bf16[262144]{0:T(1024)(128)(2,1)S(1)} %convert_element_type.610) | copy-start | bytes 1572868
  212.9 8.9 %copy-start.8 = (bf16[262144]{0:T(1024)(128)(2,1)S(1)}, bf16[262144]{0:T(1024)(128)(2,1)}, u32[]{:S(2)}) copy-start(bf16[262144]{0:T(1024)(128)(2,1)} %copy-done.7) | copy-start | bytes 1572868
  212.9 3.9 collective-permute-start.14
  214.8 6.8 %collective-permute-start.15 = (bf16[1,4,128,128]{3,2,1,0:T(8,128)(2,1)S(1)}, bf16[1,4,128,128]{3,2,1,0:T(8,128)(2,1)S(1)}, u32[]{:S(2)}, u32[]{:S(2)}) collective-permute-start(bf16[1,4,128,128]{3,2,1,0:T(8,128)(2,1)S(1)} %get-tuple-element.73), channel_id=1, source_target_pairs={{1,0},{2,1},{3,2},{4,3},{5,4},{6,5},{7,6},{9,8},{10,9},{11,10},{12... | collective-permute-start | bytes 393224 | tf_op jit(solution)/shard_map/ppermute | solution.py:29
  230.6 1.2 copy-start.6
  230.6 1.4 copy-start.9
  230.6 1.5 copy-start.11
  230.7 0.8 copy-start.13
  232.2 3.2 copy-start.12
Sparse Core Ops, SparseCore 0:
  235.5 294.5 all-reduce.10
where the time goes:
time: 548 us; the launch traced here: 540 us
  waiting for transfers between devices  315 us (57%)
  other arithmetic  109 us (20%)
  local copies, waits for them, and re-layouts  47.4 us (9%)
  starting transfers between devices  42.6 us (8%)
  between operations  25.6 us (5%)
    psum x1, waiting for transfers between devices, body(): summed = lax.psum(gradient, 'shot')  292 us
    convert_element_type x4, other arithmetic, body(): inject(updated, source_ids, wavelet[:, moment:moment + 1], anchor)  44.6 us
    gather x4, local copies, waits for them, and re-layouts, record(): jnp.take_along_axis(wavefield.reshape(shot_count, -1), flat_index, axis=1)  38.5 us
    ppermute x8, starting transfers between devices, padded_2(): lax.ppermute(tail, axis, [(i, (i + 1) % count) for i in range(ends)])  32.1 us
    unnamed x7, other arithmetic  26.2 us
    ppermute x8, waiting for transfers between devices, padded_2(): lax.ppermute(head, axis, [((i + 1) % count, i) for i in range(ends)])  20.1 us
    convert_element_type x4, other arithmetic, body(): images.append(laplacian.astype(jnp.bfloat16))  12.2 us
  transfers between devices with their start and end apart: 17, of which 9 were waited for; matrix products, arithmetic and copies ran while one was open for 16% of the time, Pallas kernels for 0%

commit v1 on v0

--- a/solution.py
+++ b/solution.py
@@ -123,7 +123,7 @@
         )
         farther, nearer = (nearer, updated)
     step_scale = step_base / math.sqrt(forward_start.shape[1] * lax.axis_size("shot"))
-    summed = lax.psum(gradient, "shot")
+    summed = jnp.sum(lax.all_gather(gradient, "shot"), axis=0)
     velocity_new = jnp.clip(velocity - step_scale * summed, low_speed, high_speed)
     forward_end = jnp.stack([earlier, current])
     adjoint_start = jnp.stack([nearer, farther])

time: 548 us -> 475 us (0.87)
  waiting for transfers between devices: 315 us -> 230 us
  other arithmetic: 109 us -> 120 us
    psum x1 -> x0, waiting for transfers between devices: 292 us -> none  [body(): summed = lax.psum(gradient, 'shot')]
    all_gather x0 -> x1, waiting for transfers between devices: none -> 208 us  [body(): summed = jnp.sum(lax.all_gather(gradient, 'shot'), axis=0)]
    reduce_sum x0 -> x1, other arithmetic: none -> 11.7 us  [body(): summed = jnp.sum(lax.all_gather(gradient, 'shot'), axis=0)]
  transfers between devices with their start and end apart: 17 -> 17, of which waited for: 9 -> 9; matrix products, arithmetic and copies ran while one was open for 16% -> 18% of each run, Pallas kernels for 0% -> 0%
where the time goes in v1:
time: 475 us; the launch traced here: 466 us
  waiting for transfers between devices  230 us (48%)
  other arithmetic  120 us (25%)
  local copies, waits for them, and re-layouts  47.4 us (10%)
  starting transfers between devices  42.6 us (9%)
  between operations  25.6 us (5%)
    all_gather x1, waiting for transfers between devices, body(): summed = jnp.sum(lax.all_gather(gradient, 'shot'), axis=0)  208 us
    convert_element_type x4, other arithmetic, body(): inject(updated, source_ids, wavelet[:, moment:moment + 1], anchor)  44.6 us
    gather x4, local copies, waits for them, and re-layouts, record(): jnp.take_along_axis(wavefield.reshape(shot_count, -1), flat_index, axis=1)  38.5 us
    ppermute x8, starting transfers between devices, padded_2(): lax.ppermute(tail, axis, [(i, (i + 1) % count) for i in range(ends)])  32.1 us
    unnamed x7, other arithmetic  26.2 us
    ppermute x8, waiting for transfers between devices, padded_2(): lax.ppermute(head, axis, [((i + 1) % count, i) for i in range(ends)])  20.1 us
    convert_element_type x4, other arithmetic, body(): images.append(laplacian.astype(jnp.bfloat16))  12.2 us
    reduce_sum x1, other arithmetic, body(): summed = jnp.sum(lax.all_gather(gradient, 'shot'), axis=0)  11.7 us
  transfers between devices with their start and end apart: 17, of which 9 were waited for; matrix products, arithmetic and copies ran while one was open for 18% of the time, Pallas kernels for 0%

profile of v1, /device:TPU:1, one launch (start us, length us, event | category | flops | bytes accessed | tf_op | source)
XLA Modules:
  0.0 465.6 jit_solution(2141525029654058160)
XLA Ops:
  7.3 1.2 slice_bitcast_fusion.1
  8.5 4.4 collective-permute-start
  12.8 1.3 collective-permute-start.1
  14.2 0.8 copy-done.20
  15.0 0.7 fusion.228
  15.7 4.0 collective-permute-start.8
  19.7 1.3 collective-permute-start.9
  21.2 0.7 fusion.233
  25.0 0.8 and_reduce_fusion.1
  26.1 3.0 fusion.222
  29.4 0.6 fusion.234
  32.0 10.9 %convert_reduce_fusion.3 = bf16[262144]{0:T(1024)(128)(2,1)S(1)} fusion(f32[1,262144]{1,0:T(1,128)S(1)} %scatter-add.48), kind=kLoop, calls=%fused_computation.412 | loop fusion | flops 262144 | bytes 1572864 | tf_op jit(solution)/shard_map/convert_element_type | solution.py:104
  42.9 4.2 collective-permute-start.2
  47.1 1.3 collective-permute-start.3
  48.4 0.6 collective-permute-done.2
  49.0 5.8 %collective-permute-done.3 = bf16[1,4,128,128]{3,2,1,0:T(8,128)(2,1)S(1)} collective-permute-done((bf16[1,4,128,128]{3,2,1,0:T(8,128)(2,1)S(1)}, bf16[1,4,128,128]{3,2,1,0:T(8,128)(2,1)S(1)}, u32[]{:S(2)}, u32[]{:S(2)}) %collective-permute-start.3) | collective-permute-done | bytes 131104 | tf_op jit(solution)/shard_map/ppermute | solution.py:29
  54.9 3.1 fusion.220
  58.3 0.6 fusion.235
  61.3 10.9 %convert_reduce_fusion.2 = bf16[262144]{0:T(1024)(128)(2,1)S(1)} fusion(f32[1,262144]{1,0:T(1,128)S(1)} %scatter-add.49), kind=kLoop, calls=%fused_computation.411 | loop fusion | flops 262144 | bytes 1572864 | tf_op jit(solution)/shard_map/convert_element_type | solution.py:104
  72.2 3.2 collective-permute-start.4
  75.4 1.3 collective-permute-start.5
  76.7 11.4 %gather_fusion.3 = bf16[1024]{0:T(1024)(128)(2,1)} fusion(bf16[262144]{0:T(1024)(128)(2,1)S(1)} %convert_reduce_fusion.3, s32[1024]{0:T(1024)S(1)} %broadcast_clamp_fusion), kind=kCustom, calls=%fused_computation.3.clone | custom fusion | bytes 8192 | tf_op jit(solution)/shard_map/jit(take_along_axis)/gather | solution.py:85
  88.3 3.1 fusion.218
  91.6 0.7 fusion.236
  94.3 10.9 %convert_reduce_fusion.1 = bf16[262144]{0:T(1024)(128)(2,1)S(1)} fusion(f32[1,262144]{1,0:T(1,128)S(1)} %scatter-add.50), kind=kLoop, calls=%fused_computation.410 | loop fusion | flops 262144 | bytes 1572864 | tf_op jit(solution)/shard_map/convert_element_type | solution.py:104
  105.2 0.7 fusion.229
  105.9 4.0 collective-permute-start.6
  109.9 1.5 collective-permute-start.7
  111.4 1.2 maximum_convert_fusion.4
  112.6 13.5 %gather_fusion.2 = bf16[1024]{0:T(1024)(128)(2,1)S(1)} fusion(bf16[262144]{0:T(1024)(128)(2,1)} %copy-done.1, s32[1024]{0:T(1024)S(1)} %broadcast_clamp_fusion), kind=kCustom, calls=%fused_computation.2.clone | custom fusion | bytes 8192 | tf_op jit(solution)/shard_map/jit(take_along_axis)/gather | solution.py:85
  126.1 6.8 %gather_fusion.1 = bf16[1024]{0:T(1024)(128)(2,1)S(1)} fusion(bf16[262144]{0:T(1024)(128)(2,1)S(1)} %convert_reduce_fusion.1, s32[1024]{0:T(1024)S(1)} %broadcast_clamp_fusion), kind=kCustom, calls=%fused_computation.1.clone | custom fusion | bytes 8192 | tf_op jit(solution)/shard_map/jit(take_along_axis)/gather | solution.py:85
  132.9 1.0 maximum_convert_fusion.3
  134.0 3.1 fusion.216
  137.0 3.4 fusion.6
  140.5 1.0 copy-done.14
  141.4 0.6 fusion.237
  143.9 1.3 scatter-add.51
  145.2 12.0 %convert_reduce_fusion = bf16[262144]{0:T(1024)(128)(2,1)S(1)} fusion(f32[1,262144]{1,0:T(1,128)} %scatter-add.51), kind=kLoop, calls=%fused_computation.409 | loop fusion | flops 262144 | bytes 1572864 | tf_op jit(solution)/shard_map/convert_element_type | solution.py:104
  157.1 6.8 %gather_fusion = bf16[1024]{0:T(1024)(128)(2,1)S(1)} fusion(bf16[262144]{0:T(1024)(128)(2,1)S(1)} %convert_reduce_fusion, s32[1024]{0:T(1024)S(1)} %broadcast_clamp_fusion), kind=kCustom, calls=%fused_computation.clone | custom fusion | bytes 8192 | tf_op jit(solution)/shard_map/jit(take_along_axis)/gather | solution.py:85
  164.0 6.5 %scatter_fusion = f32[262144]{0:T(1024)S(1)} fusion(f32[262144]{0:T(1024)S(1)} %bitcast.98, s32[1024]{0:T(1024)S(1)} %broadcast_select_fusion, f32[1024]{0:T(1024)S(1)} %bitcast.134), kind=kCustom, calls=%fused_computation.4 | custom fusion | flops 1024 | bytes 16384
  170.6 4.9 %collective-permute-start.10 = (bf16[1,4,128,128]{3,2,1,0:T(8,128)(2,1)S(1)}, bf16[1,4,128,128]{3,2,1,0:T(8,128)(2,1)S(1)}, u32[]{:S(2)}, u32[]{:S(2)}) collective-permute-start(bf16[1,4,128,128]{3,2,1,0:T(8,128)(2,1)S(1)} %get-tuple-element.76), channel_id=1, source_target_pairs={{0,1},{1,2},{2,3},{3,4},{4,5},{5,6},{6,7},{8,9},{9,10},{10,11},{11... | collective-permute-start | bytes 393224 | tf_op jit(solution)/shard_map/ppermute | solution.py:27
  175.6 1.3 collective-permute-start.11
  176.9 0.6 collective-permute-done.10
  177.5 4.7 %collective-permute-done.11 = bf16[1,4,128,128]{3,2,1,0:T(8,128)(2,1)S(1)} collective-permute-done((bf16[1,4,128,128]{3,2,1,0:T(8,128)(2,1)S(1)}, bf16[1,4,128,128]{3,2,1,0:T(8,128)(2,1)S(1)}, u32[]{:S(2)}, u32[]{:S(2)}) %collective-permute-start.11) | collective-permute-done | bytes 131104 | tf_op jit(solution)/shard_map/ppermute | solution.py:29
  182.3 2.4 fusion.7
  184.7 6.7 %scatter_fusion.1 = f32[262144]{0:T(1024)S(1)} fusion(f32[262144]{0:T(1024)S(1)} %bitcast.100, s32[1024]{0:T(1024)S(1)} %broadcast_select_fusion, f32[1024]{0:T(1024)S(1)} %bitcast.133), kind=kCustom, calls=%fused_computation.5 | custom fusion | flops 1024 | bytes 16384
  191.5 5.5 %collective-permute-start.12 = (bf16[1,4,128,128]{3,2,1,0:T(8,128)(2,1)S(1)}, bf16[1,4,128,128]{3,2,1,0:T(8,128)(2,1)S(1)}, u32[]{:S(2)}, u32[]{:S(2)}) collective-permute-start(bf16[1,4,128,128]{3,2,1,0:T(8,128)(2,1)S(1)} %get-tuple-element.74), channel_id=1, source_target_pairs={{0,1},{1,2},{2,3},{3,4},{4,5},{5,6},{6,7},{8,9},{9,10},{10,11},{11... | collective-permute-start | bytes 393224 | tf_op jit(solution)/shard_map/ppermute | solution.py:27
  197.0 1.3 collective-permute-start.13
  198.3 0.6 collective-permute-done.12
  198.9 4.8 %collective-permute-done.13 = bf16[1,4,128,128]{3,2,1,0:T(8,128)(2,1)S(1)} collective-permute-done((bf16[1,4,128,128]{3,2,1,0:T(8,128)(2,1)S(1)}, bf16[1,4,128,128]{3,2,1,0:T(8,128)(2,1)S(1)}, u32[]{:S(2)}, u32[]{:S(2)}) %collective-permute-start.13) | collective-permute-done | bytes 131104 | tf_op jit(solution)/shard_map/ppermute | solution.py:29
  203.9 2.4 fusion.10
  206.3 6.5 %scatter_fusion.2 = f32[262144]{0:T(1024)S(1)} fusion(f32[262144]{0:T(1024)S(1)} %bitcast.101, s32[1024]{0:T(1024)S(1)} %broadcast_select_fusion, f32[1024]{0:T(1024)S(1)} %bitcast.132), kind=kCustom, calls=%fused_computation.6 | custom fusion | flops 1024 | bytes 16384
  212.9 1.9 collective-permute-start.14
  214.8 1.3 collective-permute-start.15
  216.1 0.6 collective-permute-done.14
  216.8 4.8 %collective-permute-done.15 = bf16[1,4,128,128]{3,2,1,0:T(8,128)(2,1)S(1)} collective-permute-done((bf16[1,4,128,128]{3,2,1,0:T(8,128)(2,1)S(1)}, bf16[1,4,128,128]{3,2,1,0:T(8,128)(2,1)S(1)}, u32[]{:S(2)}, u32[]{:S(2)}) %collective-permute-start.15) | collective-permute-done | bytes 131104 | tf_op jit(solution)/shard_map/ppermute | solution.py:29
  221.7 2.4 fusion.12
  224.2 6.5 %scatter_fusion.3 = f32[262144]{0:T(1024)S(1)} fusion(f32[262144]{0:T(1024)S(1)} %bitcast.99, s32[1024]{0:T(1024)S(1)} %broadcast_select_fusion, f32[1024]{0:T(1024)S(1)} %bitcast.131), kind=kCustom, calls=%fused_computation.7 | custom fusion | flops 1024 | bytes 16384
  230.7 0.8 copy-done.13
  232.2 3.2 fusion.9
  235.4 2.5 pad_maximum_fusion
  237.9 207.8 %all-gather.2.cloned.1.call-done = f32[32,16,128,128]{3,2,1,0:T(8,128)} async-done(((f32[1,16,128,128]{3,2,1,0:T(8,128)}), f32[32,16,128,128]{3,2,1,0:T(8,128)}) %all-gather.2.cloned.1.call-update) | async-done | bytes 33554448 | tf_op jit(solution)/shard_map/all_gather | solution.py:126
  445.7 11.7 %reduce_sum.8 = f32[16,128,128]{2,1,0:T(8,128)S(1)} reduce(f32[32,16,128,128]{3,2,1,0:T(8,128)} %all-gather.2.cloned.1.call-done, f32[]{:T(128)} %constant.221.clone.1), dimensions={0}, to_apply=%region_5.7 | reduce | flops 8126464 | bytes 34603012 | tf_op jit(solution)/shard_map/reduce_sum | solution.py:126
  457.4 1.1 subtract_clamp_fusion
  (90 shorter events, 3.9 us)
Async XLA Ops:
  7.2 13.9 %copy-start.26 = (s32[2]{0:T(128)S(1)}, s32[2]{0:T(128)}, u32[]{:S(2)}) copy-start(s32[2]{0:T(128)} %constant.279) | copy-start | bytes 28
  7.2 18.6 %copy-start.25 = (s32[2]{0:T(128)S(1)}, s32[2]{0:T(128)}, u32[]{:S(2)}) copy-start(s32[2]{0:T(128)} %constant.276) | copy-start | bytes 28
  7.2 6.9 %copy-start.15 = (bf16[2,1,16,128,128]{4,3,2,1,0:T(8,128)(2,1)S(1)}, bf16[2,1,16,128,128]{4,3,2,1,0:T(8,128)(2,1)}, u32[]{:S(2)}) copy-start(bf16[2,1,16,128,128]{4,3,2,1,0:T(8,128)(2,1)} %param.18) | copy-start | bytes 3145732
  7.2 13.8 %copy-start.24 = (s32[1,1024]{1,0:T(1,128)S(1)}, s32[1,1024]{1,0:T(1,128)}, u32[]{:S(2)}) copy-start(s32[1,1024]{1,0:T(1,128)} %param.22) | copy-start | bytes 12292
  7.2 14.0 %copy-start.23 = (f32[1,4]{1,0:T(1,128)S(1)}, f32[1,4]{1,0:T(1,128)}, u32[]{:S(2)}) copy-start(f32[1,4]{1,0:T(1,128)} %param.21) | copy-start | bytes 52
  7.2 438.5 %all-gather.2.cloned.1.call-start = ((), (), s32[]{:S(2)}) async-start(), calls=%async_computation | async-start | bytes 34603008 | tf_op jit(solution)/shard_map/all_gather | solution.py:126
  8.5 17.4 %collective-permute-start = (bf16[1,4,128,128]{3,2,1,0:T(8,128)(2,1)S(1)}, bf16[1,4,128,128]{3,2,1,0:T(8,128)(2,1)S(1)}, u32[]{:S(2)}, u32[]{:S(2)}) collective-permute-start(bf16[1,4,128,128]{3,2,1,0:T(8,128)(2,1)S(1)} %get-tuple-element.86), channel_id=1, source_target_pairs={{0,1},{1,2},{2,3},{3,4},{4,5},{5,6},{6,7},{8,9},{9,10},{10,11},{11... | collective-permute-start | bytes 393224 | tf_op jit(solution)/shard_map/ppermute | solution.py:27
  12.8 13.1 %collective-permute-start.1 = (bf16[1,4,128,128]{3,2,1,0:T(8,128)(2,1)S(1)}, bf16[1,4,128,128]{3,2,1,0:T(8,128)(2,1)S(1)}, u32[]{:S(2)}, u32[]{:S(2)}) collective-permute-start(bf16[1,4,128,128]{3,2,1,0:T(8,128)(2,1)S(1)} %get-tuple-element.87), channel_id=1, source_target_pairs={{1,0},{2,1},{3,2},{4,3},{5,4},{6,5},{7,6},{9,8},{10,9},{11,10},{12... | collective-permute-start | bytes 393224 | tf_op jit(solution)/shard_map/ppermute | solution.py:29
  14.2 0.8 copy-start.20
  15.7 95.7 %collective-permute-start.8 = (bf16[1,4,128,128]{3,2,1,0:T(8,128)(2,1)}, bf16[1,4,128,128]{3,2,1,0:T(8,128)(2,1)S(1)}, u32[]{:S(2)}, u32[]{:S(2)}) collective-permute-start(bf16[1,4,128,128]{3,2,1,0:T(8,128)(2,1)} %get-tuple-element.78), channel_id=1, source_target_pairs={{0,1},{1,2},{2,3},{3,4},{4,5},{5,6},{6,7},{8,9},{9,10},{10,11},{11... | collective-permute-start | bytes 393224 | tf_op jit(solution)/shard_map/ppermute | solution.py:27
  19.7 91.7 %collective-permute-start.9 = (bf16[1,4,128,128]{3,2,1,0:T(8,128)(2,1)}, bf16[1,4,128,128]{3,2,1,0:T(8,128)(2,1)S(1)}, u32[]{:S(2)}, u32[]{:S(2)}) collective-permute-start(bf16[1,4,128,128]{3,2,1,0:T(8,128)(2,1)} %get-tuple-element.79), channel_id=1, source_target_pairs={{1,0},{2,1},{3,2},{4,3},{5,4},{6,5},{7,6},{9,8},{10,9},{11,10},{12... | collective-permute-start | bytes 393224 | tf_op jit(solution)/shard_map/ppermute | solution.py:29
  26.0 3.1 copy-start
  26.1 3.1 copy-start.18
  42.9 6.1 %collective-permute-start.2 = (bf16[1,4,128,128]{3,2,1,0:T(8,128)(2,1)S(1)}, bf16[1,4,128,128]{3,2,1,0:T(8,128)(2,1)S(1)}, u32[]{:S(2)}, u32[]{:S(2)}) collective-permute-start(bf16[1,4,128,128]{3,2,1,0:T(8,128)(2,1)S(1)} %get-tuple-element.84), channel_id=1, source_target_pairs={{0,1},{1,2},{2,3},{3,4},{4,5},{5,6},{6,7},{8,9},{9,10},{10,11},{11... | collective-permute-start | bytes 393224 | tf_op jit(solution)/shard_map/ppermute | solution.py:27
  47.1 7.7 %collective-permute-start.3 = (bf16[1,4,128,128]{3,2,1,0:T(8,128)(2,1)S(1)}, bf16[1,4,128,128]{3,2,1,0:T(8,128)(2,1)S(1)}, u32[]{:S(2)}, u32[]{:S(2)}) collective-permute-start(bf16[1,4,128,128]{3,2,1,0:T(8,128)(2,1)S(1)} %get-tuple-element.85), channel_id=1, source_target_pairs={{1,0},{2,1},{3,2},{4,3},{5,4},{6,5},{7,6},{9,8},{10,9},{11,10},{12... | collective-permute-start | bytes 393224 | tf_op jit(solution)/shard_map/ppermute | solution.py:29
  54.9 3.1 copy-start.19
  72.2 19.2 %copy-start.1 = (bf16[262144]{0:T(1024)(128)(2,1)}, bf16[262144]{0:T(1024)(128)(2,1)S(1)}, u32[]{:S(2)}) copy-start(bf16[262144]{0:T(1024)(128)(2,1)S(1)} %convert_reduce_fusion.2) | copy-start | bytes 1572868
  72.2 15.9 %collective-permute-start.4 = (bf16[1,4,128,128]{3,2,1,0:T(8,128)(2,1)S(1)}, bf16[1,4,128,128]{3,2,1,0:T(8,128)(2,1)S(1)}, u32[]{:S(2)}, u32[]{:S(2)}) collective-permute-start(bf16[1,4,128,128]{3,2,1,0:T(8,128)(2,1)S(1)} %get-tuple-element.82), channel_id=1, source_target_pairs={{0,1},{1,2},{2,3},{3,4},{4,5},{5,6},{6,7},{8,9},{9,10},{10,11},{11... | collective-permute-start | bytes 393224 | tf_op jit(solution)/shard_map/ppermute | solution.py:27
  75.4 12.7 %collective-permute-start.5 = (bf16[1,4,128,128]{3,2,1,0:T(8,128)(2,1)S(1)}, bf16[1,4,128,128]{3,2,1,0:T(8,128)(2,1)S(1)}, u32[]{:S(2)}, u32[]{:S(2)}) collective-permute-start(bf16[1,4,128,128]{3,2,1,0:T(8,128)(2,1)S(1)} %get-tuple-element.83), channel_id=1, source_target_pairs={{1,0},{2,1},{3,2},{4,3},{5,4},{6,5},{7,6},{9,8},{10,9},{11,10},{12... | collective-permute-start | bytes 393224 | tf_op jit(solution)/shard_map/ppermute | solution.py:29
  105.9 27.0 %collective-permute-start.6 = (bf16[1,4,128,128]{3,2,1,0:T(8,128)(2,1)}, bf16[1,4,128,128]{3,2,1,0:T(8,128)(2,1)S(1)}, u32[]{:S(2)}, u32[]{:S(2)}) collective-permute-start(bf16[1,4,128,128]{3,2,1,0:T(8,128)(2,1)} %get-tuple-element.80), channel_id=1, source_target_pairs={{0,1},{1,2},{2,3},{3,4},{4,5},{5,6},{6,7},{8,9},{9,10},{10,11},{11... | collective-permute-start | bytes 393224 | tf_op jit(solution)/shard_map/ppermute | solution.py:27
  109.9 23.0 %collective-permute-start.7 = (bf16[1,4,128,128]{3,2,1,0:T(8,128)(2,1)}, bf16[1,4,128,128]{3,2,1,0:T(8,128)(2,1)}, u32[]{:S(2)}, u32[]{:S(2)}) collective-permute-start(bf16[1,4,128,128]{3,2,1,0:T(8,128)(2,1)} %get-tuple-element.81), channel_id=1, source_target_pairs={{1,0},{2,1},{3,2},{4,3},{5,4},{6,5},{7,6},{9,8},{10,9},{11,10},{12... | collective-permute-start | bytes 393224 | tf_op jit(solution)/shard_map/ppermute | solution.py:29
  133.9 3.1 copy-start.2
  133.9 3.1 copy-start.16
  140.5 1.0 copy-start.14
  145.1 18.8 %copy-start.21 = (f32[1,4,1024]{2,1,0:T(4,128)S(1)}, f32[1,4,1024]{2,1,0:T(4,128)}, u32[]{:S(2)}) copy-start(f32[1,4,1024]{2,1,0:T(4,128)} %param.23) | copy-start | bytes 49156
  145.2 18.8 %copy-start.22 = (bf16[1024]{0:T(1024)(128)(2,1)S(1)}, bf16[1024]{0:T(1024)(128)(2,1)}, u32[]{:S(2)}) copy-start(bf16[1024]{0:T(1024)(128)(2,1)} %gather_fusion.3) | copy-start | bytes 6148
  145.2 18.9 %copy-start.3 = (f32[1,16,128,128]{3,2,1,0:T(8,128)S(1)}, f32[1,16,128,128]{3,2,1,0:T(8,128)}, u32[]{:S(2)}) copy-start(f32[1,16,128,128]{3,2,1,0:T(8,128)} %get-tuple-element.70) | copy-start | bytes 3145732
  170.6 14.1 %copy-start.4 = (bf16[262144]{0:T(1024)(128)(2,1)}, bf16[262144]{0:T(1024)(128)(2,1)S(1)}, u32[]{:S(2)}) copy-start(bf16[262144]{0:T(1024)(128)(2,1)S(1)} %convert_element_type.608) | copy-start | bytes 1572868
  170.6 11.7 %copy-start.17 = (bf16[2,1,16,128,128]{4,3,2,1,0:T(8,128)(2,1)S(1)}, bf16[2,1,16,128,128]{4,3,2,1,0:T(8,128)(2,1)}, u32[]{:S(2)}) copy-start(bf16[2,1,16,128,128]{4,3,2,1,0:T(8,128)(2,1)} %param.18) | copy-start | bytes 3145732
  170.6 6.9 %collective-permute-start.10 = (bf16[1,4,128,128]{3,2,1,0:T(8,128)(2,1)S(1)}, bf16[1,4,128,128]{3,2,1,0:T(8,128)(2,1)S(1)}, u32[]{:S(2)}, u32[]{:S(2)}) collective-permute-start(bf16[1,4,128,128]{3,2,1,0:T(8,128)(2,1)S(1)} %get-tuple-element.76), channel_id=1, source_target_pairs={{0,1},{1,2},{2,3},{3,4},{4,5},{5,6},{6,7},{8,9},{9,10},{10,11},{11... | collective-permute-start | bytes 393224 | tf_op jit(solution)/shard_map/ppermute | solution.py:27
  175.6 6.6 %collective-permute-start.11 = (bf16[1,4,128,128]{3,2,1,0:T(8,128)(2,1)S(1)}, bf16[1,4,128,128]{3,2,1,0:T(8,128)(2,1)S(1)}, u32[]{:S(2)}, u32[]{:S(2)}) collective-permute-start(bf16[1,4,128,128]{3,2,1,0:T(8,128)(2,1)S(1)} %get-tuple-element.77), channel_id=1, source_target_pairs={{1,0},{2,1},{3,2},{4,3},{5,4},{6,5},{7,6},{9,8},{10,9},{11,10},{12... | collective-permute-start | bytes 393224 | tf_op jit(solution)/shard_map/ppermute | solution.py:29
  191.5 14.9 %copy-start.7 = (bf16[262144]{0:T(1024)(128)(2,1)}, bf16[262144]{0:T(1024)(128)(2,1)S(1)}, u32[]{:S(2)}) copy-start(bf16[262144]{0:T(1024)(128)(2,1)S(1)} %convert_element_type.609) | copy-start | bytes 1572868
  191.5 12.4 %copy-start.5 = (bf16[262144]{0:T(1024)(128)(2,1)S(1)}, bf16[262144]{0:T(1024)(128)(2,1)}, u32[]{:S(2)}) copy-start(bf16[262144]{0:T(1024)(128)(2,1)} %copy-done.4) | copy-start | bytes 1572868
  191.5 7.4 %collective-permute-start.12 = (bf16[1,4,128,128]{3,2,1,0:T(8,128)(2,1)S(1)}, bf16[1,4,128,128]{3,2,1,0:T(8,128)(2,1)S(1)}, u32[]{:S(2)}, u32[]{:S(2)}) collective-permute-start(bf16[1,4,128,128]{3,2,1,0:T(8,128)(2,1)S(1)} %get-tuple-element.74), channel_id=1, source_target_pairs={{0,1},{1,2},{2,3},{3,4},{4,5},{5,6},{6,7},{8,9},{9,10},{10,11},{11... | collective-permute-start | bytes 393224 | tf_op jit(solution)/shard_map/ppermute | solution.py:27
  197.0 6.7 %collective-permute-start.13 = (bf16[1,4,128,128]{3,2,1,0:T(8,128)(2,1)S(1)}, bf16[1,4,128,128]{3,2,1,0:T(8,128)(2,1)S(1)}, u32[]{:S(2)}, u32[]{:S(2)}) collective-permute-start(bf16[1,4,128,128]{3,2,1,0:T(8,128)(2,1)S(1)} %get-tuple-element.75), channel_id=1, source_target_pairs={{1,0},{2,1},{3,2},{4,3},{5,4},{6,5},{7,6},{9,8},{10,9},{11,10},{12... | collective-permute-start | bytes 393224 | tf_op jit(solution)/shard_map/ppermute | solution.py:29
  212.9 11.3 %copy-start.10 = (bf16[262144]{0:T(1024)(128)(2,1)}, bf16[262144]{0:T(1024)(128)(2,1)S(1)}, u32[]{:S(2)}) copy-start(bf16[262144]{0:T(1024)(128)(2,1)S(1)} %convert_element_type.610) | copy-start | bytes 1572868
  212.9 8.9 %copy-start.8 = (bf16[262144]{0:T(1024)(128)(2,1)S(1)}, bf16[262144]{0:T(1024)(128)(2,1)}, u32[]{:S(2)}) copy-start(bf16[262144]{0:T(1024)(128)(2,1)} %copy-done.7) | copy-start | bytes 1572868
  212.9 3.9 collective-permute-start.14
  214.8 6.8 %collective-permute-start.15 = (bf16[1,4,128,128]{3,2,1,0:T(8,128)(2,1)S(1)}, bf16[1,4,128,128]{3,2,1,0:T(8,128)(2,1)S(1)}, u32[]{:S(2)}, u32[]{:S(2)}) collective-permute-start(bf16[1,4,128,128]{3,2,1,0:T(8,128)(2,1)S(1)} %get-tuple-element.73), channel_id=1, source_target_pairs={{1,0},{2,1},{3,2},{4,3},{5,4},{6,5},{7,6},{9,8},{10,9},{11,10},{12... | collective-permute-start | bytes 393224 | tf_op jit(solution)/shard_map/ppermute | solution.py:29
  230.6 1.2 copy-start.6
  230.6 1.4 copy-start.9
  230.6 1.5 copy-start.11
  230.7 0.8 copy-start.13
  232.2 3.2 copy-start.12
Sparse Core Ops, SparseCore 0:
  235.5 210.1 all-gather.1
